TPU v7x, 128 devices: a whole 4x4x4 slice. The times are simulated.
128 devices in a mesh: dp: 16 (over z, y_lo, core), space: 8 (over x, y_hi).
Axes of the slice: x: 4, y: 4 (y_hi: 2, y_lo: 2; y = y_hi * 2 + y_lo), z: 4, core: 2. Of those that a mesh axis runs over, the one named last changes fastest.
Arguments:
- decoder_input: bfloat16 [16, 64, 16, 16, 128], P('dp', None, 'space'), may hold values from -6 to 6
- cotangent: bfloat16 [16, 64, 16, 16, 128], P('dp', None, 'space'), may hold values from -6 to 6
- encoder_input: bfloat16 [16, 64, 16, 16, 128], P('dp', None, 'space'), may hold values from -6 to 6
- decoder_weights: bfloat16 [2, 27, 4096], replicated, may hold values from -0.15625 to 0.15625
- other_grads: bfloat16 [16, 8, 12, 27, 4096], P('dp', 'space'), may hold values from -384 to 384
- assignment: int32 [12], replicated, may hold values from 0 to 31, as said below
- moment_first: float32 [32, 27, 4096], P('dp', None, 'space'), may hold values from -4 to 4
- moment_second: float32 [32, 27, 4096], P('dp', None, 'space'), may hold values from 0.02 to 2
- master_weights: float32 [32, 27, 4096], P('dp', None, 'space'), may hold values from -0.15625 to 0.15625
Outputs:
- input_grad: bfloat16 [16, 64, 16, 16, 128], P('dp', None, 'space')
- encoder_out: bfloat16 [16, 64, 16, 16, 128], P('dp', None, 'space')
- new_params: bfloat16 [12, 27, 4096], replicated
- new_first: float32 [32, 27, 4096], P('dp', None, 'space')
- new_second: float32 [32, 27, 4096], P('dp', None, 'space')
- new_master: float32 [32, 27, 4096], P('dp', None, 'space')
Inputs may be any that keep to these rules, and one draw needn't show every extreme that they name: `assignment`: the values are distinct; value j places the tensor with owner j // 2 in that owner's slot j % 2; some owner holds 2 tensors.
All inputs are finite; a program needn't handle non-finite values.
Results may differ from a plain program's by a relative error of at most 0.005.
Values may be sent and summed in bfloat16 or wider, within the bound.
No kernel may reach another device: no remote copies, remote signals or barrier semaphores. Data moves between devices by JAX's collectives and lax.ppermute only.
A program may use at most 128 MiB of HBM per device.

v0:
```python
import math
import jax
import jax.numpy as jnp
from jax import lax
from jax.sharding import PartitionSpec as P

learn_rate = 0.002
decay_rate = 0.1
epsilon = 1e-08
bias_one = 1.0 - (0.9**50) ** 2
bias_two = 1.0 - (0.999**50) ** 2
volume_dims = ("NCDHW", "OIDHW", "NCDHW")
swapped_dims = ("CNDHW", "OIDHW", "NCDHW")


def padded_2(block, sides, width):
    for axis, dim in sides:
        count = lax.axis_size(axis)
        forward = [(i, i + 1) for i in range(count - 1)]
        forward.append((count - 1, 0))
        backward = [(target, source) for source, target in forward]
        low = lax.ppermute(
            lax.slice_in_dim(block, block.shape[dim] - width, None, axis=dim), axis, forward
        )
        high = lax.ppermute(lax.slice_in_dim(block, 0, width, axis=dim), axis, backward)
        block = jnp.concatenate([low, block, high], axis=dim)
    return block


def widened(field):
    rimmed = padded_2(field, (("space", 1),), 1)
    return jnp.pad(rimmed, ((0, 0), (0, 0), (1, 1), (1, 1)), mode="wrap")


def forward_local(padded, kernel):
    channels = kernel.shape[1]
    weights = kernel.reshape(3, 3, 3, channels, channels).transpose(3, 4, 0, 1, 2)
    result = lax.conv_general_dilated(
        padded[None],
        weights,
        (1, 1, 1),
        "VALID",
        dimension_numbers=volume_dims,
        preferred_element_type=jnp.float32,
    )
    return result[0].reshape(channels, -1)


def backward_local(padded, kernel):
    channels = kernel.shape[1]
    weights = kernel.reshape(3, 3, 3, channels, channels)[::-1, ::-1, ::-1].transpose(4, 3, 0, 1, 2)
    result = lax.conv_general_dilated(
        padded[None],
        weights,
        (1, 1, 1),
        "VALID",
        dimension_numbers=volume_dims,
        preferred_element_type=jnp.float32,
    )
    return result[0].reshape(channels, -1)


def kernel_grad(grad_field, padded):
    channels = grad_field.shape[0]
    result = lax.conv_general_dilated(
        padded[None],
        grad_field[:, None],
        (1, 1, 1),
        "VALID",
        dimension_numbers=swapped_dims,
        preferred_element_type=jnp.float32,
    )
    return result.transpose(2, 3, 4, 1, 0).reshape(27, channels, channels)


def space_scatter(block):
    count = lax.axis_size("space")
    lead = block.shape[:-1]
    split = block.reshape(lead + (count, block.shape[-1] // count))
    split = jnp.moveaxis(split, -2, 0)
    return lax.psum_scatter(split, "space", scatter_dimension=0, tiled=True)[0]


def space_gather(block):
    count = lax.axis_size("space")
    lead = block.shape[:-1]
    whole = lax.all_gather(block, "space", axis=0, tiled=False)
    whole = jnp.moveaxis(whole, 0, -2)
    return whole.reshape(lead + (count * block.shape[-1],))


def adamw(grads, first, second, master):
    new_first = 0.9 * first + 0.1 * grads
    new_second = 0.999 * second + 0.001 * grads * grads
    update = new_first / bias_one / (jnp.sqrt(new_second / bias_two) + epsilon)
    new_master = master - learn_rate * (update + decay_rate * master)
    return (new_first, new_second, new_master)


def owner_rows(grads, assign, owner, first, second, master):
    slot_count = first.shape[0]
    local = assign % slot_count
    pick = lambda state: jnp.take(state, local, axis=0)
    rows = adamw(grads, pick(first), pick(second), pick(master))[2].astype(jnp.bfloat16)
    mine = (assign // slot_count == owner)[:, None, None]
    return jnp.where(mine, rows, jnp.zeros_like(rows))


def per_device(
    decoder_input,
    cotangent,
    encoder_input,
    decoder_weights,
    other_grads,
    assignment,
    moment_first,
    moment_second,
    master_weights,
):
    field_shape = decoder_input.shape[1:]
    channels = field_shape[0]
    thick = field_shape[1]
    kernel_a = decoder_weights[0].reshape(27, channels, channels)
    kernel_b = decoder_weights[1].reshape(27, channels, channels)
    dec_field = decoder_input[0]
    dec_wide = widened(dec_field)
    preact = forward_local(dec_wide, kernel_a)
    sigma = jax.nn.sigmoid(preact)
    hidden = (preact * sigma).astype(jnp.bfloat16).reshape(field_shape)
    cot_field = cotangent[0]
    grad_b = kernel_grad(cot_field, widened(hidden))
    grad_hidden = backward_local(widened(cot_field), kernel_b)
    grad_pre = (
        (grad_hidden * sigma * (1.0 + preact * (1.0 - sigma)))
        .astype(jnp.bfloat16)
        .reshape(field_shape)
    )
    grad_a = kernel_grad(grad_pre, dec_wide)
    input_grad = backward_local(widened(grad_pre), kernel_a)
    input_grad = input_grad.astype(jnp.bfloat16).reshape((1,) + field_shape)
    replicas = lax.axis_size("dp")
    slabs = lax.axis_size("space")
    scale = 1.0 / math.sqrt(replicas * thick * slabs * field_shape[2] * field_shape[3])
    owner = lax.axis_index("dp")
    other_tot = lax.psum(space_scatter(other_grads[0, 0]), "dp").astype(jnp.float32)
    enc_rows = owner_rows(
        other_tot[2:4] * scale, assignment[2:4], owner, moment_first, moment_second, master_weights
    )
    enc_params = space_gather(lax.psum(enc_rows, "dp"))
    kernel_c = enc_params[0].reshape(27, channels, channels)
    kernel_d = enc_params[1].reshape(27, channels, channels)
    ab_grads = jnp.stack([grad_a.reshape(27, -1), grad_b.reshape(27, -1)]).astype(jnp.bfloat16)
    ab_tot = lax.psum(space_scatter(ab_grads), "dp").astype(jnp.float32)
    totals = jnp.concatenate([other_tot[:2] + ab_tot, other_tot[2:]]) * scale
    slot_count = moment_first.shape[0]
    slot_ids = owner * slot_count + jnp.arange(slot_count)
    match = assignment[None, :] == slot_ids[:, None]
    owned = jnp.sum(jnp.where(match[:, :, None, None], totals[None], 0.0), axis=1)
    new_first, new_second, new_master = adamw(owned, moment_first, moment_second, master_weights)
    late = jnp.array([0, 1] + list(range(4, assignment.shape[0])))
    late_assign = assignment[late]
    late_local = jnp.take(new_master.astype(jnp.bfloat16), late_assign % slot_count, axis=0)
    late_rows = jnp.where(
        (late_assign // slot_count == owner)[:, None, None], late_local, jnp.zeros_like(late_local)
    )
    late_params = space_gather(lax.psum(late_rows, "dp"))
    new_params = jnp.concatenate([late_params[:2], enc_params, late_params[2:]])
    enc_field = encoder_input[0]
    first = forward_local(widened(enc_field), kernel_c)
    activ = (first * jax.nn.sigmoid(first)).astype(jnp.bfloat16).reshape(field_shape)
    second = forward_local(widened(activ), kernel_d)
    encoder_out = (enc_field.reshape(channels, -1).astype(jnp.float32) + second).astype(
        jnp.bfloat16
    )
    encoder_out = encoder_out.reshape((1,) + field_shape)
    return (input_grad, encoder_out, new_params, new_first, new_second, new_master)


def solution(mesh):
    in_specs = (
        P("dp", None, "space", None, None),
        P("dp", None, "space", None, None),
        P("dp", None, "space", None, None),
        P(),
        P("dp", "space", None, None, None),
        P(),
        P("dp", None, "space"),
        P("dp", None, "space"),
        P("dp", None, "space"),
    )
    out_specs = (
        P("dp", None, "space", None, None),
        P("dp", None, "space", None, None),
        P(),
        P("dp", None, "space"),
        P("dp", None, "space"),
        P("dp", None, "space"),
    )
    return jax.shard_map(
        per_device, mesh=mesh, in_specs=in_specs, out_specs=out_specs, check_vma=False
    )
```

profile of v0, /device:TPU:0, one launch (start us, length us, event | category | flops | bytes accessed | tf_op | source)
XLA Modules:
  0.0 786.5 jit_solution(13005885202175331573)
XLA Ops:
  9.1 3.3 collective-permute-start
  18.0 4.4 collective-permute-start.3
  22.4 4.7 reshape_squeeze.21
  27.2 4.5 copy.311
  51.8 5.6 collective-permute-start.7
  59.4 5.7 maximum_bitcast_fusion
  65.1 7.8 copy.231
  75.2 4.6 fusion.53
  85.1 4.6 fusion.140
  89.7 5.9 copy.232
  99.5 8.6 %fusion.50 = f32[2,16,8,17,64]{4,2,3,1,0:T(8,128)S(1)} fusion(bf16[3,3,3,64,64]{4,3,2,1,0:T(8,128)(2,1)S(1)} %copy-done.33, bf16[64,4,18,1,7,2]{0,4,5,2,1,3:T(8,128)(2,1)S(1)} %slice.228, bf16[64,4,18,1,8,17]{0,4,5,2,1,3:T(8,128)(2,1)S(1)} %copy.170, pred[8,17]{0,1:T(8,128)(4,1)S(1)} %copy-done.44), kind=kOutput, calls=%fused_computation.57 | convolution fusion | flops 967073792 | bytes 2717832 | tf_op jit(solution)/shard_map/conv_general_dilated | solution.py:38
  110.0 3.7 copy.229
  116.8 5.2 fusion.139
  125.0 9.1 %copy.202 = bf16[1,64,4,18,130]{1,0,4,3,2:T(2,128)(2,1)} copy(bf16[1,64,4,18,130]{4,1,3,2,0:T(8,128)(2,1)S(1)} %copy-done.12) | data formatting | bytes 2396160 | tf_op jit(solution)/shard_map/broadcast_in_dim | solution.py:39
  135.0 5.6 collective-permute-start.11
  148.4 30.6 %convolution_convert_fusion.1 = bf16[3,3,3,64,64]{3,4,2,1,0:T(8,128)(2,1)} fusion(bf16[1,64,4,18,130]{1,0,4,3,2:T(2,128)(2,1)S(1)} %copy-done.15, bf16[64,1,2,16,128]{0,1,4,3,2:T(2,128)(2,1)S(1)} %copy-done.24), kind=kOutput, calls=%fused_computation.66 | convolution fusion | flops 906080256 | bytes 1943552 | tf_op jit(solution)/shard_map/transpose | solution.py:73
  179.0 5.2 maximum_bitcast_fusion.1
  188.2 5.7 copy.233
  198.9 5.6 collective-permute-start.5
  208.7 9.4 %copy.208 = bf16[1,64,4,18,130]{1,0,4,3,2:T(2,128)(2,1)} copy(bf16[1,64,4,18,130]{4,1,3,2,0:T(8,128)(2,1)S(1)} %maximum_bitcast_fusion.4) | data formatting | bytes 2396160 | tf_op jit(solution)/shard_map/broadcast_in_dim | solution.py:66
  218.0 32.9 %convolution_convert_fusion = bf16[3,3,3,64,64]{3,4,2,1,0:T(8,128)(2,1)S(1)} fusion(bf16[1,64,4,18,130]{1,0,4,3,2:T(2,128)(2,1)} %copy.208, bf16[64,1,2,16,128]{0,1,4,3,2:T(2,128)(2,1)} %copy.209), kind=kOutput, calls=%fused_computation.65 | convolution fusion | flops 906080256 | bytes 1943552 | tf_op jit(solution)/shard_map/transpose | solution.py:73
  258.7 4.5 copy.234
  265.7 72.5 %all-reduce.11.cloned.1.call-done = bf16[8,2,27,512]{3,1,2,0:T(2,128)(2,1)} async-done(((bf16[8,2,27,512]{3,1,2,0:T(2,128)(2,1)}), bf16[8,2,27,512]{3,1,2,0:T(2,128)(2,1)}) %all-reduce.11.cloned.1.call-update) | async-done | bytes 442384
  340.4 116.6 %all-reduce.7.cloned.1.call-done = bf16[12,27,512]{2,1,0:T(8,128)(2,1)} async-done(((bf16[12,27,512]{2,1,0:T(8,128)(2,1)}), bf16[12,27,512]{2,1,0:T(8,128)(2,1)}) %all-reduce.7.cloned.1.call-update) | async-done | bytes 331792 | tf_op jit(solution)/shard_map/psum | solution.py:145
  460.0 5.4 select_convert_fusion
  466.6 112.2 %all-reduce.13.cloned.1.call-done = (bf16[1,2,27,512]{3,2,1,0:T(8,128)(2,1)}, bf16[2,27,512]{2,1,0:T(8,128)(2,1)}) async-done(((bf16[1,2,27,512]{3,2,1,0:T(8,128)(2,1)}, bf16[2,27,512]{2,1,0:T(8,128)(2,1)}), (bf16[1,2,27,512]{3,2,1,0:T(8,128)(2,1)}, bf16[2,27,512]{2,1,0:T(8,128)(2,1)})) %all-reduce.13.cloned.1.call-update) | async-done | bytes 110608 | tf_op jit(solution)/shard_map/psum | solution.py:149
  582.4 34.9 %all_gather.13 = bf16[8,2,27,512]{3,1,2,0:T(2,128)(2,1)S(1)} all-gather(bf16[1,2,27,512]{3,1,2,0:T(2,128)(2,1)S(1)} %copy.188), channel_id=1, replica_groups=mesh['dp'=16,'space'=8] {'space'}, dimensions={0}, use_global_device_ids=true | all-gather | bytes 497664 | tf_op jit(solution)/shard_map/all_gather | solution.py:87
  618.2 79.7 %all-reduce.9.cloned.1.call-done = bf16[1,10,27,512]{3,2,1,0:T(8,128)(2,1)} async-done(((bf16[1,10,27,512]{3,2,1,0:T(8,128)(2,1)}), bf16[1,10,27,512]{3,2,1,0:T(8,128)(2,1)}) %all-reduce.9.cloned.1.call-update) | async-done | bytes 276496 | tf_op jit(solution)/shard_map/psum | solution.py:166
  697.9 10.3 %fusion.47 = f32[2,16,8,17,64]{4,2,3,1,0:T(8,128)S(1)} fusion(bf16[3,3,3,64,64]{4,3,2,1,0:T(8,128)(2,1)S(1)} %reshape_reshape_squeeze.15, bf16[64,4,18,1,7,2]{0,4,5,2,1,3:T(8,128)(2,1)S(1)} %copy-done.35, bf16[64,4,18,1,8,17]{0,4,5,2,1,3:T(8,128)(2,1)} %copy-done.22, pred[8,17]{0,1:T(8,128)(4,1)S(1)} %copy-done.45), kind=kOutput, calls=%fused_computation.56 | convolution fusion | flops 967073792 | bytes 2717832 | tf_op jit(solution)/shard_map/conv_general_dilated | solution.py:38
  736.5 4.8 copy.235
  742.9 8.6 %fusion.42 = f32[2,16,8,17,64]{4,2,3,1,0:T(8,128)S(1)} fusion(bf16[3,3,3,64,64]{4,3,2,1,0:T(8,128)(2,1)S(1)} %reshape_reshape_squeeze.16, bf16[64,4,18,1,7,2]{0,4,5,2,1,3:T(8,128)(2,1)S(1)} %slice.252, bf16[64,4,18,1,8,17]{0,4,5,2,1,3:T(8,128)(2,1)S(1)} %copy.197, pred[8,17]{0,1:T(8,128)(4,1)S(1)} %copy-done.45), kind=kOutput, calls=%fused_computation.55 | convolution fusion | flops 967073792 | bytes 2717832 | tf_op jit(solution)/shard_map/conv_general_dilated | solution.py:38
  755.0 10.5 %all-gather.2.cloned.1.call-done = bf16[8,10,27,512]{3,2,1,0:T(8,128)(2,1)} async-done(((bf16[1,10,27,512]{3,2,1,0:T(8,128)(2,1)}), bf16[8,10,27,512]{3,2,1,0:T(8,128)(2,1)}) %all-gather.2.cloned.1.call-update) | async-done | bytes 2211856 | tf_op jit(solution)/shard_map/all_gather | solution.py:87
  (248 shorter events, 138.1 us)
Async XLA Ops:
  7.2 247.8 %reduce-scatter.2.cloned.1.call-start = ((), (), s32[]{:S(2)}) async-start(), calls=%async_computation.1 | async-start | bytes 3538944 | tf_op jit(solution)/shard_map/reduce_scatter | solution.py:81
  9.1 42.8 %collective-permute-start = (bf16[64,1,16,128]{3,2,1,0:T(8,128)(2,1)}, bf16[64,1,16,128]{3,2,1,0:T(8,128)(2,1)S(1)}, u32[]{:S(2)}, u32[]{:S(2)}) collective-permute-start(bf16[64,1,16,128]{3,2,1,0:T(8,128)(2,1)} %get-tuple-element.78), channel_id=1, source_target_pairs={{0,1},{1,2},{2,3},{3,4},{4,5},{5,6},{6,7},{7,0},{8,9},{9,10},{10,1... | collective-permute-start | bytes 786440 | tf_op jit(solution)/shard_map/ppermute | solution.py:22
  12.4 45.1 %collective-permute-start.1 = (bf16[64,1,16,128]{3,2,1,0:T(8,128)(2,1)}, bf16[64,1,16,128]{3,2,1,0:T(8,128)(2,1)S(1)}, u32[]{:S(2)}, u32[]{:S(2)}) collective-permute-start(bf16[64,1,16,128]{3,2,1,0:T(8,128)(2,1)} %get-tuple-element.79), channel_id=1, source_target_pairs={{1,0},{2,1},{3,2},{4,3},{5,4},{6,5},{7,6},{0,7},{9,8},{10,9},{11,1... | collective-permute-start | bytes 786440 | tf_op jit(solution)/shard_map/ppermute | solution.py:25
  16.8 65.7 %collective-permute-start.2 = (bf16[64,1,16,128]{3,0,2,1:T(8,128)(2,1)}, bf16[64,1,16,128]{3,0,2,1:T(8,128)(2,1)}, u32[]{:S(2)}, u32[]{:S(2)}) collective-permute-start(bf16[64,1,16,128]{3,0,2,1:T(8,128)(2,1)} %get-tuple-element.76), channel_id=1, source_target_pairs={{0,1},{1,2},{2,3},{3,4},{4,5},{5,6},{6,7},{7,0},{8,9},{9,10},{10,1... | collective-permute-start | bytes 786440 | tf_op jit(solution)/shard_map/ppermute | solution.py:22
  18.0 64.5 %collective-permute-start.3 = (bf16[64,1,16,128]{3,0,2,1:T(8,128)(2,1)}, bf16[64,1,16,128]{3,0,2,1:T(8,128)(2,1)}, u32[]{:S(2)}, u32[]{:S(2)}) collective-permute-start(bf16[64,1,16,128]{3,0,2,1:T(8,128)(2,1)} %get-tuple-element.77), channel_id=1, source_target_pairs={{1,0},{2,1},{3,2},{4,3},{5,4},{6,5},{7,6},{0,7},{9,8},{10,9},{11,1... | collective-permute-start | bytes 786440 | tf_op jit(solution)/shard_map/ppermute | solution.py:25
  31.7 306.6 %all-reduce.11.cloned.1.call-start = ((), (), s32[]{:S(2)}) async-start(), calls=%async_computation.5 | async-start | bytes 884736
  33.5 107.1 %collective-permute-start.6 = (bf16[64,1,16,128]{3,2,1,0:T(8,128)(2,1)}, bf16[64,1,16,128]{3,2,1,0:T(8,128)(2,1)}, u32[]{:S(2)}, u32[]{:S(2)}) collective-permute-start(bf16[64,1,16,128]{3,2,1,0:T(8,128)(2,1)} %get-tuple-element.70), channel_id=1, source_target_pairs={{0,1},{1,2},{2,3},{3,4},{4,5},{5,6},{6,7},{7,0},{8,9},{9,10},{10,1... | collective-permute-start | bytes 786440 | tf_op jit(solution)/shard_map/ppermute | solution.py:22
  51.8 88.8 %collective-permute-start.7 = (bf16[64,1,16,128]{3,2,1,0:T(8,128)(2,1)}, bf16[64,1,16,128]{3,2,1,0:T(8,128)(2,1)}, u32[]{:S(2)}, u32[]{:S(2)}) collective-permute-start(bf16[64,1,16,128]{3,2,1,0:T(8,128)(2,1)} %get-tuple-element.71), channel_id=1, source_target_pairs={{1,0},{2,1},{3,2},{4,3},{5,4},{6,5},{7,6},{0,7},{9,8},{10,9},{11,1... | collective-permute-start | bytes 786440 | tf_op jit(solution)/shard_map/ppermute | solution.py:25
  135.0 69.5 %collective-permute-start.10 = (bf16[64,1,16,128]{3,2,1,0:T(8,128)(2,1)}, bf16[64,1,16,128]{3,2,1,0:T(8,128)(2,1)}, u32[]{:S(2)}, u32[]{:S(2)}) collective-permute-start(bf16[64,1,16,128]{3,2,1,0:T(8,128)(2,1)} %get-tuple-element.72), channel_id=1, source_target_pairs={{0,1},{1,2},{2,3},{3,4},{4,5},{5,6},{6,7},{7,0},{8,9},{9,10},{10,1... | collective-permute-start | bytes 786440 | tf_op jit(solution)/shard_map/ppermute | solution.py:22
  135.0 69.5 %collective-permute-start.11 = (bf16[64,1,16,128]{3,2,1,0:T(8,128)(2,1)}, bf16[64,1,16,128]{3,2,1,0:T(8,128)(2,1)}, u32[]{:S(2)}, u32[]{:S(2)}) collective-permute-start(bf16[64,1,16,128]{3,2,1,0:T(8,128)(2,1)} %get-tuple-element.73), channel_id=1, source_target_pairs={{1,0},{2,1},{3,2},{4,3},{5,4},{6,5},{7,6},{0,7},{9,8},{10,9},{11,1... | collective-permute-start | bytes 786440 | tf_op jit(solution)/shard_map/ppermute | solution.py:25
  148.4 30.6 %copy-start.29 = (bf16[64,4,1,128]{3,2,1,0:T(2,128)(2,1)S(1)}, bf16[64,4,1,128]{3,2,1,0:T(2,128)(2,1)}, u32[]{:S(2)}) copy-start(bf16[64,4,1,128]{3,2,1,0:T(2,128)(2,1)} %copy-done.28) | copy-start | bytes 196612
  198.9 53.8 %collective-permute-start.4 = (bf16[64,1,16,128]{3,2,1,0:T(8,128)(2,1)}, bf16[64,1,16,128]{3,2,1,0:T(8,128)(2,1)}, u32[]{:S(2)}, u32[]{:S(2)}) collective-permute-start(bf16[64,1,16,128]{3,2,1,0:T(8,128)(2,1)} %get-tuple-element.74), channel_id=1, source_target_pairs={{0,1},{1,2},{2,3},{3,4},{4,5},{5,6},{6,7},{7,0},{8,9},{9,10},{10,1... | collective-permute-start | bytes 786440 | tf_op jit(solution)/shard_map/ppermute | solution.py:22
  198.9 53.8 %collective-permute-start.5 = (bf16[64,1,16,128]{3,2,1,0:T(8,128)(2,1)}, bf16[64,1,16,128]{3,2,1,0:T(8,128)(2,1)}, u32[]{:S(2)}, u32[]{:S(2)}) collective-permute-start(bf16[64,1,16,128]{3,2,1,0:T(8,128)(2,1)} %get-tuple-element.75), channel_id=1, source_target_pairs={{1,0},{2,1},{3,2},{4,3},{5,4},{6,5},{7,6},{0,7},{9,8},{10,9},{11,1... | collective-permute-start | bytes 786440 | tf_op jit(solution)/shard_map/ppermute | solution.py:25
  218.0 33.5 %copy-start.30 = (bf16[1,27,8,512]{3,2,1,0:T(8,128)(2,1)S(1)}, bf16[1,27,8,512]{3,2,1,0:T(8,128)(2,1)}, u32[]{:S(2)}) copy-start(bf16[1,27,8,512]{3,2,1,0:T(8,128)(2,1)} %stack.7) | copy-start | bytes 663556
  254.1 202.9 %all-reduce.7.cloned.1.call-start = ((), (), s32[]{:S(2)}) async-start(), calls=%async_computation.2 | async-start | bytes 786432 | tf_op jit(solution)/shard_map/psum | solution.py:145
  255.0 323.9 %all-reduce.13.cloned.1.call-start = ((), (), s32[]{:S(2)}) async-start(), calls=%async_computation.6 | async-start | bytes 262144 | tf_op jit(solution)/shard_map/psum | solution.py:149
  264.5 193.5 %copy-start.31 = (f32[2,27,512]{2,0,1:T(2,128)S(1)}, f32[2,27,512]{2,0,1:T(2,128)}, u32[]{:S(2)}) copy-start(f32[2,27,512]{2,0,1:T(2,128)} %gather_fusion.2) | copy-start | bytes 331780
  264.6 193.5 %copy-start.32 = (f32[2,27,512]{2,0,1:T(2,128)S(1)}, f32[2,27,512]{2,0,1:T(2,128)}, u32[]{:S(2)}) copy-start(f32[2,27,512]{2,0,1:T(2,128)} %gather_fusion.3) | copy-start | bytes 331780
  264.6 193.5 %copy-start.40 = (pred[2]{0:T(512)(128)(4,1)S(1)}, pred[2]{0:T(512)(128)(4,1)}, u32[]{:S(2)}) copy-start(pred[2]{0:T(512)(128)(4,1)} %get-tuple-element.39) | copy-start | bytes 10
  264.6 193.5 %copy-start.41 = (pred[2]{0:T(512)(128)(4,1)S(1)}, pred[2]{0:T(512)(128)(4,1)}, u32[]{:S(2)}) copy-start(pred[2]{0:T(512)(128)(4,1)} %fusion.99) | copy-start | bytes 10
  264.9 195.0 %copy-start.45 = (pred[8,17]{0,1:T(8,128)(4,1)S(1)}, pred[8,17]{0,1:T(8,128)(4,1)}, u32[]{:S(2)}) copy-start(pred[8,17]{0,1:T(8,128)(4,1)} %constant.141) | copy-start | bytes 412
  459.9 238.0 %all-reduce.9.cloned.1.call-start = ((), (), s32[]{:S(2)}) async-start(), calls=%async_computation.3 | async-start | bytes 655360 | tf_op jit(solution)/shard_map/psum | solution.py:166
  465.4 114.4 %copy-start.37 = (pred[2,12]{0,1:T(8,128)(4,1)S(1)}, pred[2,12]{0,1:T(8,128)(4,1)}, u32[]{:S(2)}) copy-start(pred[2,12]{0,1:T(8,128)(4,1)} %broadcast_compare_fusion) | copy-start | bytes 76
  466.5 113.9 %copy-start.5 = (f32[2,27,512]{2,0,1:T(2,128)S(1)}, f32[2,27,512]{2,0,1:T(2,128)}, u32[]{:S(2)}) copy-start(f32[2,27,512]{2,0,1:T(2,128)} %param.19) | copy-start | bytes 331780
  466.5 113.9 %copy-start.7 = (f32[2,27,512]{2,0,1:T(2,128)S(1)}, f32[2,27,512]{2,0,1:T(2,128)}, u32[]{:S(2)}) copy-start(f32[2,27,512]{2,0,1:T(2,128)} %param.18) | copy-start | bytes 331780
  466.5 114.0 %copy-start.9 = (f32[2,27,512]{2,0,1:T(2,128)S(1)}, f32[2,27,512]{2,0,1:T(2,128)}, u32[]{:S(2)}) copy-start(f32[2,27,512]{2,0,1:T(2,128)} %param.20) | copy-start | bytes 331780
  466.6 114.7 %copy-start.38 = (pred[10]{0:T(512)(128)(4,1)S(1)}, pred[10]{0:T(512)(128)(4,1)}, u32[]{:S(2)}) copy-start(pred[10]{0:T(512)(128)(4,1)} %get-tuple-element.82) | copy-start | bytes 34
  466.6 114.7 %copy-start.39 = (pred[10]{0:T(512)(128)(4,1)S(1)}, pred[10]{0:T(512)(128)(4,1)}, u32[]{:S(2)}) copy-start(pred[10]{0:T(512)(128)(4,1)} %get-tuple-element.83) | copy-start | bytes 34
  581.4 116.6 %copy-start.35 = (bf16[64,4,18,1,7,2]{0,4,5,2,1,3:T(8,128)(2,1)S(1)}, bf16[64,4,18,1,7,2]{0,4,5,2,1,3:T(8,128)(2,1)}, u32[]{:S(2)}) copy-start(bf16[64,4,18,1,7,2]{0,4,5,2,1,3:T(8,128)(2,1)} %slice.242) | copy-start | bytes 387076
  582.2 183.3 %all-gather.2.cloned.1.call-start = ((), (), s32[]{:S(2)}) async-start(), calls=%async_computation.4 | async-start | bytes 2949120 | tf_op jit(solution)/shard_map/all_gather | solution.py:87
  713.4 14.5 %collective-permute-start.8 = (bf16[64,1,16,128]{3,2,1,0:T(8,128)(2,1)}, bf16[64,1,16,128]{3,2,1,0:T(8,128)(2,1)}, u32[]{:S(2)}, u32[]{:S(2)}) collective-permute-start(bf16[64,1,16,128]{3,2,1,0:T(8,128)(2,1)} %get-tuple-element.68), channel_id=1, source_target_pairs={{0,1},{1,2},{2,3},{3,4},{4,5},{5,6},{6,7},{7,0},{8,9},{9,10},{10,1... | collective-permute-start | bytes 786440 | tf_op jit(solution)/shard_map/ppermute | solution.py:22
  716.2 14.8 %collective-permute-start.9 = (bf16[64,1,16,128]{3,2,1,0:T(8,128)(2,1)S(1)}, bf16[64,1,16,128]{3,2,1,0:T(8,128)(2,1)}, u32[]{:S(2)}, u32[]{:S(2)}) collective-permute-start(bf16[64,1,16,128]{3,2,1,0:T(8,128)(2,1)S(1)} %get-tuple-element.69), channel_id=1, source_target_pairs={{1,0},{2,1},{3,2},{4,3},{5,4},{6,5},{7,6},{0,7},{9,8},{10,9},{11,1... | collective-permute-start | bytes 786440 | tf_op jit(solution)/shard_map/ppermute | solution.py:25
  (32 other events, 237.7 us)
Sparse Core Ops, SparseCore 0:
  31.8 85.4 reduce-scatter.1
  254.2 83.9 all-reduce.10
  340.7 116.2 all-reduce.6
  460.0 118.7 all-reduce.12
  582.3 115.5 all-reduce.8
  700.1 65.3 all-gather.1
where the time goes:
time: 797 us; the launch traced here: 786 us
  waiting for transfers between devices  395 us (50%)
  local copies, waits for them, and re-layouts  150 us (19%)
  matrix products  101 us (13%)
  other arithmetic  54.6 us (7%)
  blocking collectives  34.9 us (4%)
  starting transfers between devices  34.5 us (4%)
  between operations  15.6 us (2%)
    psum x1, waiting for transfers between devices, per_device(): lax.psum(space_scatter(other_grads[0, 0]), 'dp').astype(jnp.float32)  117 us
    psum x1, waiting for transfers between devices, per_device(): enc_params = space_gather(lax.psum(enc_rows, 'dp'))  112 us
    psum x1, waiting for transfers between devices, per_device(): late_params = space_gather(lax.psum(late_rows, 'dp'))  79.7 us
    unnamed x7, waiting for transfers between devices  72.6 us
    transpose x2, matrix products, kernel_grad(): return result.transpose(2, 3, 4, 1, 0).reshape(27, channels, channels)  63.5 us
    unnamed x116, local copies, waits for them, and re-layouts  60.2 us
    all_gather x1, blocking collectives, space_gather(): whole = lax.all_gather(block, 'space', axis=0, tiled=False)  34.9 us
    conv_general_dilated x3, matrix products, forward_local(): lax.conv_general_dilated(padded[None], weights, (1, 1, 1), 'VALID', dimen...  27.5 us
  transfers between devices with their start and end apart: 18, of which 7 were waited for; matrix products, arithmetic and copies ran while one was open for 36% of the time, Pallas kernels for 0%

commit v1 on v0

--- a/solution.py
+++ b/solution.py
@@ -146,7 +146,7 @@
     enc_rows = owner_rows(
         other_tot[2:4] * scale, assignment[2:4], owner, moment_first, moment_second, master_weights
     )
-    enc_params = space_gather(lax.psum(enc_rows, "dp"))
+    enc_params = space_gather(jnp.sum(lax.all_gather(enc_rows, "dp"), 0))
     kernel_c = enc_params[0].reshape(27, channels, channels)
     kernel_d = enc_params[1].reshape(27, channels, channels)
     ab_grads = jnp.stack([grad_a.reshape(27, -1), grad_b.reshape(27, -1)]).astype(jnp.bfloat16)

time: 797 us -> 683 us (0.86)
  waiting for transfers between devices: 395 us -> 205 us
  blocking collectives: 34.9 us -> 109 us
    psum x1 -> x0, waiting for transfers between devices: 112 us -> none  [per_device(): enc_params = space_gather(lax.psum(enc_rows, 'dp'))]
    psum x0 -> x1, blocking collectives: none -> 53.1 us  [per_device(): ab_tot = lax.psum(space_scatter(ab_grads), 'dp').astype(jnp.float32)]
    psum x1, waiting for transfers between devices: 117 us -> 64.3 us  [per_device(): lax.psum(space_scatter(other_grads[0, 0]), 'dp').astype(jnp.float32)]
    psum x1, waiting for transfers between devices: 79.7 us -> 57 us  [per_device(): late_params = space_gather(lax.psum(late_rows, 'dp'))]
    all_gather x0 -> x1, blocking collectives: none -> 21.1 us  [per_device(): enc_params = space_gather(jnp.sum(lax.all_gather(enc_rows, 'dp'), 0))]
    unnamed x7 -> x6, waiting for transfers between devices: 72.6 us -> 68.1 us
    unnamed x116 -> x114, local copies, waits for them, and re-layouts: 60.2 us -> 60.9 us
  transfers between devices with their start and end apart: 18 -> 17, of which waited for: 7 -> 6; matrix products, arithmetic and copies ran while one was open for 36% -> 42% of each run, Pallas kernels for 0% -> 0%
where the time goes in v1:
time: 683 us; the launch traced here: 673 us
  waiting for transfers between devices  205 us (30%)
  local copies, waits for them, and re-layouts  154 us (23%)
  blocking collectives  109 us (16%)
  matrix products  99.9 us (15%)
  other arithmetic  55.8 us (8%)
  starting transfers between devices  34.5 us (5%)
  between operations  15.3 us (2%)
    unnamed x6, waiting for transfers between devices  68.1 us
    psum x1, waiting for transfers between devices, per_device(): lax.psum(space_scatter(other_grads[0, 0]), 'dp').astype(jnp.float32)  64.3 us
    transpose x2, matrix products, kernel_grad(): return result.transpose(2, 3, 4, 1, 0).reshape(27, channels, channels)  63.5 us
    unnamed x114, local copies, waits for them, and re-layouts  60.9 us
    psum x1, waiting for transfers between devices, per_device(): late_params = space_gather(lax.psum(late_rows, 'dp'))  57 us
    psum x1, blocking collectives, per_device(): ab_tot = lax.psum(space_scatter(ab_grads), 'dp').astype(jnp.float32)  53.1 us
    all_gather x1, blocking collectives, space_gather(): whole = lax.all_gather(block, 'space', axis=0, tiled=False)  35.1 us
    conv_general_dilated x3, matrix products, forward_local(): lax.conv_general_dilated(padded[None], weights, (1, 1, 1), 'VALID', dimen...  27.5 us
  transfers between devices with their start and end apart: 17, of which 6 were waited for; matrix products, arithmetic and copies ran while one was open for 42% of the time, Pallas kernels for 0%

profile of v1, /device:TPU:0, one launch (start us, length us, event | category | flops | bytes accessed | tf_op | source)
XLA Modules:
  0.0 672.9 jit_solution(5166762640945628211)
XLA Ops:
  18.0 4.4 collective-permute-start.3
  22.4 3.4 reshape_squeeze.21
  48.8 5.6 collective-permute-start.7
  58.3 6.6 maximum_bitcast_fusion
  64.8 7.8 %copy.261 = bf16[64,4,18,1,130]{0,1,4,2,3:T(4,128)(2,1)S(1)} copy(bf16[64,4,18,1,130]{4,2,1,0,3:T(8,128)(2,1)} %maximum_bitcast_fusion) | data formatting | bytes 2396160
  74.9 4.6 fusion.53
  84.8 4.7 fusion.139
  89.5 5.9 copy.262
  99.4 8.6 %fusion.50 = f32[2,16,8,17,64]{4,2,3,1,0:T(8,128)S(1)} fusion(bf16[3,3,3,64,64]{4,3,2,1,0:T(8,128)(2,1)S(1)} %copy-done.32, bf16[64,4,18,1,7,2]{0,4,5,2,1,3:T(8,128)(2,1)S(1)} %slice.228, bf16[64,4,18,1,8,17]{0,4,5,2,1,3:T(8,128)(2,1)S(1)} %copy.202, pred[8,17]{0,1:T(8,128)(4,1)S(1)} %copy-done.43), kind=kOutput, calls=%fused_computation.57 | convolution fusion | flops 967073792 | bytes 2717832 | tf_op jit(solution)/shard_map/conv_general_dilated | solution.py:38
  109.9 3.7 copy.259
  119.1 5.6 collective-permute-start.11
  124.8 4.4 copy.233
  129.1 4.6 fusion.138
  133.7 12.1 %copy.232 = bf16[1,64,4,18,130]{1,0,4,3,2:T(2,128)(2,1)} copy(bf16[1,64,4,18,130]{4,1,3,2,0:T(8,128)(2,1)} %fusion.138) | data formatting | bytes 2396160 | tf_op jit(solution)/shard_map/broadcast_in_dim | solution.py:39
  153.5 30.6 %convolution_convert_fusion.1 = bf16[3,3,3,64,64]{3,4,2,1,0:T(8,128)(2,1)} fusion(bf16[1,64,4,18,130]{1,0,4,3,2:T(2,128)(2,1)S(1)} %copy-done.14, bf16[64,1,2,16,128]{0,1,4,3,2:T(2,128)(2,1)S(1)} %copy-done.22), kind=kOutput, calls=%fused_computation.66 | convolution fusion | flops 906080256 | bytes 1943552 | tf_op jit(solution)/shard_map/transpose | solution.py:73
  184.2 5.2 maximum_bitcast_fusion.1
  193.4 5.7 copy.263
  204.1 5.6 collective-permute-start.5
  213.9 9.3 %copy.238 = bf16[1,64,4,18,130]{1,0,4,3,2:T(2,128)(2,1)} copy(bf16[1,64,4,18,130]{4,1,3,2,0:T(8,128)(2,1)S(1)} %maximum_bitcast_fusion.4) | data formatting | bytes 2396160 | tf_op jit(solution)/shard_map/broadcast_in_dim | solution.py:66
  223.2 32.9 %convolution_convert_fusion = bf16[3,3,3,64,64]{3,4,2,1,0:T(8,128)(2,1)S(1)} fusion(bf16[1,64,4,18,130]{1,0,4,3,2:T(2,128)(2,1)} %copy.238, bf16[64,1,2,16,128]{0,1,4,3,2:T(2,128)(2,1)} %copy.239), kind=kOutput, calls=%fused_computation.65 | convolution fusion | flops 906080256 | bytes 1943552 | tf_op jit(solution)/shard_map/transpose | solution.py:73
  263.8 4.5 copy.264
  270.6 4.3 select_convert_fusion
  276.1 68.0 %all-reduce.9.cloned.1.call-done = bf16[8,2,27,512]{3,1,2,0:T(2,128)(2,1)} async-done(((bf16[8,2,27,512]{3,1,2,0:T(2,128)(2,1)}), bf16[8,2,27,512]{3,1,2,0:T(2,128)(2,1)}) %all-reduce.9.cloned.1.call-update) | async-done | bytes 442384
  345.5 53.1 %psum.22 = bf16[2,27,512]{2,1,0:T(8,128)(2,1)S(1)} all-reduce(bf16[2,27,512]{2,1,0:T(8,128)(2,1)S(1)} %bitcast.211), channel_id=1, replica_groups=mesh['dp'=16,'space'=8] {'dp'}, use_global_device_ids=true, to_apply=%region_4.6 | all-reduce | flops 27648 | bytes 110592 | tf_op jit(solution)/shard_map/psum | solution.py:153
  398.6 64.3 %all-reduce.5.cloned.1.call-done = bf16[12,27,512]{2,1,0:T(8,128)(2,1)} async-done(((bf16[12,27,512]{2,1,0:T(8,128)(2,1)}), bf16[12,27,512]{2,1,0:T(8,128)(2,1)}) %all-reduce.5.cloned.1.call-update) | async-done | bytes 331792 | tf_op jit(solution)/shard_map/psum | solution.py:145
  467.9 21.1 %all-gather = bf16[32,27,512]{2,1,0:T(8,128)(2,1)S(1)} all-gather(bf16[2,27,512]{2,1,0:T(8,128)(2,1)S(1)} %broadcast_select_fusion), channel_id=2, replica_groups=mesh['dp'=16,'space'=8] {'dp'}, dimensions={0}, use_global_device_ids=true | all-gather | bytes 940032 | tf_op jit(solution)/shard_map/all_gather | solution.py:149
  489.2 35.1 %all-gather.1 = bf16[16,27,512]{2,1,0:T(8,128)(2,1)S(1)} all-gather(bf16[2,27,512]{2,1,0:T(8,128)(2,1)S(1)} %reduce_sum.21), channel_id=3, replica_groups=mesh['dp'=16,'space'=8] {'space'}, dimensions={0}, use_global_device_ids=true | all-gather | bytes 497664 | tf_op jit(solution)/shard_map/all_gather | solution.py:87
  526.9 57.0 %all-reduce.7.cloned.1.call-done = bf16[1,10,27,512]{3,2,1,0:T(8,128)(2,1)} async-done(((bf16[1,10,27,512]{3,2,1,0:T(8,128)(2,1)}), bf16[1,10,27,512]{3,2,1,0:T(8,128)(2,1)}) %all-reduce.7.cloned.1.call-update) | async-done | bytes 276496 | tf_op jit(solution)/shard_map/psum | solution.py:166
  583.9 10.3 %fusion.47 = f32[2,16,8,17,64]{4,2,3,1,0:T(8,128)S(1)} fusion(bf16[3,3,3,64,64]{4,3,2,1,0:T(8,128)(2,1)S(1)} %reshape_reshape_squeeze.15, bf16[64,4,18,1,7,2]{0,4,5,2,1,3:T(8,128)(2,1)S(1)} %copy-done.35, bf16[64,4,18,1,8,17]{0,4,5,2,1,3:T(8,128)(2,1)} %copy-done.21, pred[8,17]{0,1:T(8,128)(4,1)S(1)} %copy-done.44), kind=kOutput, calls=%fused_computation.56 | convolution fusion | flops 967073792 | bytes 2717832 | tf_op jit(solution)/shard_map/conv_general_dilated | solution.py:38
  621.8 4.9 copy.265
  628.4 8.6 %fusion.42 = f32[2,16,8,17,64]{4,2,3,1,0:T(8,128)S(1)} fusion(bf16[3,3,3,64,64]{4,3,2,1,0:T(8,128)(2,1)S(1)} %reshape_reshape_squeeze.16, bf16[64,4,18,1,7,2]{0,4,5,2,1,3:T(8,128)(2,1)S(1)} %slice.252, bf16[64,4,18,1,8,17]{0,4,5,2,1,3:T(8,128)(2,1)S(1)} %copy.228, pred[8,17]{0,1:T(8,128)(4,1)S(1)} %copy-done.44), kind=kOutput, calls=%fused_computation.55 | convolution fusion | flops 967073792 | bytes 2717832 | tf_op jit(solution)/shard_map/conv_general_dilated | solution.py:38
  640.5 11.6 %all-gather.4.cloned.1.call-done = bf16[8,10,27,512]{3,2,1,0:T(8,128)(2,1)} async-done(((bf16[1,10,27,512]{3,2,1,0:T(8,128)(2,1)}), bf16[8,10,27,512]{3,2,1,0:T(8,128)(2,1)}) %all-gather.4.cloned.1.call-update) | async-done | bytes 2211856 | tf_op jit(solution)/shard_map/all_gather | solution.py:87
  (244 shorter events, 143.7 us)
Async XLA Ops:
  7.2 262.9 %reduce-scatter.2.cloned.1.call-start = ((), (), s32[]{:S(2)}) async-start(), calls=%async_computation.1 | async-start | bytes 3538944 | tf_op jit(solution)/shard_map/reduce_scatter | solution.py:81
  9.1 39.7 %collective-permute-start = (bf16[64,1,16,128]{3,2,1,0:T(8,128)(2,1)}, bf16[64,1,16,128]{3,2,1,0:T(8,128)(2,1)S(1)}, u32[]{:S(2)}, u32[]{:S(2)}) collective-permute-start(bf16[64,1,16,128]{3,2,1,0:T(8,128)(2,1)} %get-tuple-element.84), channel_id=1, source_target_pairs={{0,1},{1,2},{2,3},{3,4},{4,5},{5,6},{6,7},{7,0},{8,9},{9,10},{10,1... | collective-permute-start | bytes 786440 | tf_op jit(solution)/shard_map/ppermute | solution.py:22
  12.4 42.0 %collective-permute-start.1 = (bf16[64,1,16,128]{3,2,1,0:T(8,128)(2,1)}, bf16[64,1,16,128]{3,2,1,0:T(8,128)(2,1)}, u32[]{:S(2)}, u32[]{:S(2)}) collective-permute-start(bf16[64,1,16,128]{3,2,1,0:T(8,128)(2,1)} %get-tuple-element.85), channel_id=1, source_target_pairs={{1,0},{2,1},{3,2},{4,3},{5,4},{6,5},{7,6},{0,7},{9,8},{10,9},{11,1... | collective-permute-start | bytes 786440 | tf_op jit(solution)/shard_map/ppermute | solution.py:25
  16.8 65.5 %collective-permute-start.2 = (bf16[64,1,16,128]{3,0,2,1:T(8,128)(2,1)}, bf16[64,1,16,128]{3,0,2,1:T(8,128)(2,1)}, u32[]{:S(2)}, u32[]{:S(2)}) collective-permute-start(bf16[64,1,16,128]{3,0,2,1:T(8,128)(2,1)} %get-tuple-element.82), channel_id=1, source_target_pairs={{0,1},{1,2},{2,3},{3,4},{4,5},{5,6},{6,7},{7,0},{8,9},{9,10},{10,1... | collective-permute-start | bytes 786440 | tf_op jit(solution)/shard_map/ppermute | solution.py:22
  18.0 64.3 %collective-permute-start.3 = (bf16[64,1,16,128]{3,0,2,1:T(8,128)(2,1)}, bf16[64,1,16,128]{3,0,2,1:T(8,128)(2,1)}, u32[]{:S(2)}, u32[]{:S(2)}) collective-permute-start(bf16[64,1,16,128]{3,0,2,1:T(8,128)(2,1)} %get-tuple-element.83), channel_id=1, source_target_pairs={{1,0},{2,1},{3,2},{4,3},{5,4},{6,5},{7,6},{0,7},{9,8},{10,9},{11,1... | collective-permute-start | bytes 786440 | tf_op jit(solution)/shard_map/ppermute | solution.py:25
  28.7 315.4 %all-reduce.9.cloned.1.call-start = ((), (), s32[]{:S(2)}) async-start(), calls=%async_computation.5 | async-start | bytes 884736
  30.5 9.6 %copy-start.1 = (bf16[1,64,2,16,128]{4,3,2,1,0:T(8,128)(2,1)S(1)}, bf16[1,64,2,16,128]{4,3,2,1,0:T(8,128)(2,1)}, u32[]{:S(2)}) copy-start(bf16[1,64,2,16,128]{4,3,2,1,0:T(8,128)(2,1)} %param.13) | copy-start | bytes 1572868
  30.5 115.3 %collective-permute-start.6 = (bf16[64,1,16,128]{3,2,1,0:T(8,128)(2,1)}, bf16[64,1,16,128]{3,2,1,0:T(8,128)(2,1)}, u32[]{:S(2)}, u32[]{:S(2)}) collective-permute-start(bf16[64,1,16,128]{3,2,1,0:T(8,128)(2,1)} %get-tuple-element.78), channel_id=1, source_target_pairs={{0,1},{1,2},{2,3},{3,4},{4,5},{5,6},{6,7},{7,0},{8,9},{9,10},{10,1... | collective-permute-start | bytes 786440 | tf_op jit(solution)/shard_map/ppermute | solution.py:22
  40.1 7.4 %copy-start.42 = (u32[128]{0:T(128)S(1)}, u32[128]{0:T(128)}, u32[]{:S(2)}) copy-start(u32[128]{0:T(128)} %constant.154) | copy-start | bytes 1540
  48.8 97.0 %collective-permute-start.7 = (bf16[64,1,16,128]{3,2,1,0:T(8,128)(2,1)}, bf16[64,1,16,128]{3,2,1,0:T(8,128)(2,1)}, u32[]{:S(2)}, u32[]{:S(2)}) collective-permute-start(bf16[64,1,16,128]{3,2,1,0:T(8,128)(2,1)} %get-tuple-element.79), channel_id=1, source_target_pairs={{1,0},{2,1},{3,2},{4,3},{5,4},{6,5},{7,6},{0,7},{9,8},{10,9},{11,1... | collective-permute-start | bytes 786440 | tf_op jit(solution)/shard_map/ppermute | solution.py:25
  119.1 90.6 %collective-permute-start.10 = (bf16[64,1,16,128]{3,2,1,0:T(8,128)(2,1)}, bf16[64,1,16,128]{3,2,1,0:T(8,128)(2,1)}, u32[]{:S(2)}, u32[]{:S(2)}) collective-permute-start(bf16[64,1,16,128]{3,2,1,0:T(8,128)(2,1)} %get-tuple-element.74), channel_id=1, source_target_pairs={{0,1},{1,2},{2,3},{3,4},{4,5},{5,6},{6,7},{7,0},{8,9},{9,10},{10,1... | collective-permute-start | bytes 786440 | tf_op jit(solution)/shard_map/ppermute | solution.py:22
  119.1 90.6 %collective-permute-start.11 = (bf16[64,1,16,128]{3,2,1,0:T(8,128)(2,1)}, bf16[64,1,16,128]{3,2,1,0:T(8,128)(2,1)}, u32[]{:S(2)}, u32[]{:S(2)}) collective-permute-start(bf16[64,1,16,128]{3,2,1,0:T(8,128)(2,1)} %get-tuple-element.75), channel_id=1, source_target_pairs={{1,0},{2,1},{3,2},{4,3},{5,4},{6,5},{7,6},{0,7},{9,8},{10,9},{11,1... | collective-permute-start | bytes 786440 | tf_op jit(solution)/shard_map/ppermute | solution.py:25
  153.5 30.6 %copy-start.3 = (bf16[1,64,2,16,128]{4,3,2,1,0:T(8,128)(2,1)S(1)}, bf16[1,64,2,16,128]{4,3,2,1,0:T(8,128)(2,1)}, u32[]{:S(2)}) copy-start(bf16[1,64,2,16,128]{4,3,2,1,0:T(8,128)(2,1)} %param.14) | copy-start | bytes 1572868
  153.5 30.6 %copy-start.12 = (bf16[64,4,18,1]{3,2,1,0:T(8,128)(2,1)S(1)}, bf16[64,4,18,1]{3,2,1,0:T(8,128)(2,1)}, u32[]{:S(2)}) copy-start(bf16[64,4,18,1]{3,2,1,0:T(8,128)(2,1)} %get-tuple-element.48) | copy-start | bytes 27652
  153.5 30.7 %copy-start.13 = (bf16[64,4,18,1]{3,2,1,0:T(8,128)(2,1)S(1)}, bf16[64,4,18,1]{3,2,1,0:T(8,128)(2,1)}, u32[]{:S(2)}) copy-start(bf16[64,4,18,1]{3,2,1,0:T(8,128)(2,1)} %get-tuple-element.49) | copy-start | bytes 27652
  153.5 30.7 %copy-start.25 = (bf16[64,4,1,128]{3,2,1,0:T(2,128)(2,1)S(1)}, bf16[64,4,1,128]{3,2,1,0:T(2,128)(2,1)}, u32[]{:S(2)}) copy-start(bf16[64,4,1,128]{3,2,1,0:T(2,128)(2,1)} %copy-done.24) | copy-start | bytes 196612
  153.5 30.7 %copy-start.27 = (bf16[64,4,1,128]{3,2,1,0:T(2,128)(2,1)S(1)}, bf16[64,4,1,128]{3,2,1,0:T(2,128)(2,1)}, u32[]{:S(2)}) copy-start(bf16[64,4,1,128]{3,2,1,0:T(2,128)(2,1)} %copy-done.26) | copy-start | bytes 196612
  202.0 7.8 %copy-start.18 = (bf16[64,2,16,128]{3,2,1,0:T(8,128)(2,1)S(1)}, bf16[64,2,16,128]{3,2,1,0:T(8,128)(2,1)}, u32[]{:S(2)}) copy-start(bf16[64,2,16,128]{3,2,1,0:T(8,128)(2,1)} %copy-done.17) | copy-start | bytes 1572868
  202.3 8.8 %copy-start.21 = (bf16[64,4,18,1,8,17]{0,4,5,2,1,3:T(8,128)(2,1)}, bf16[64,4,18,1,8,17]{0,4,5,2,1,3:T(8,128)(2,1)S(1)}, u32[]{:S(2)}) copy-start(bf16[64,4,18,1,8,17]{0,4,5,2,1,3:T(8,128)(2,1)S(1)} %copy.215) | copy-start | bytes 3760132
  204.1 53.8 %collective-permute-start.4 = (bf16[64,1,16,128]{3,2,1,0:T(8,128)(2,1)}, bf16[64,1,16,128]{3,2,1,0:T(8,128)(2,1)}, u32[]{:S(2)}, u32[]{:S(2)}) collective-permute-start(bf16[64,1,16,128]{3,2,1,0:T(8,128)(2,1)} %get-tuple-element.80), channel_id=1, source_target_pairs={{0,1},{1,2},{2,3},{3,4},{4,5},{5,6},{6,7},{7,0},{8,9},{9,10},{10,1... | collective-permute-start | bytes 786440 | tf_op jit(solution)/shard_map/ppermute | solution.py:22
  204.1 53.8 %collective-permute-start.5 = (bf16[64,1,16,128]{3,2,1,0:T(8,128)(2,1)}, bf16[64,1,16,128]{3,2,1,0:T(8,128)(2,1)}, u32[]{:S(2)}, u32[]{:S(2)}) collective-permute-start(bf16[64,1,16,128]{3,2,1,0:T(8,128)(2,1)} %get-tuple-element.81), channel_id=1, source_target_pairs={{1,0},{2,1},{3,2},{4,3},{5,4},{6,5},{7,6},{0,7},{9,8},{10,9},{11,1... | collective-permute-start | bytes 786440 | tf_op jit(solution)/shard_map/ppermute | solution.py:25
  223.2 33.5 %copy-start.28 = (bf16[1,27,8,512]{3,2,1,0:T(8,128)(2,1)S(1)}, bf16[1,27,8,512]{3,2,1,0:T(8,128)(2,1)}, u32[]{:S(2)}) copy-start(bf16[1,27,8,512]{3,2,1,0:T(8,128)(2,1)} %stack.7) | copy-start | bytes 663556
  260.0 202.8 %all-reduce.5.cloned.1.call-start = ((), (), s32[]{:S(2)}) async-start(), calls=%async_computation.2 | async-start | bytes 786432 | tf_op jit(solution)/shard_map/psum | solution.py:145
  270.1 313.7 %all-reduce.7.cloned.1.call-start = ((), (), s32[]{:S(2)}) async-start(), calls=%async_computation.3 | async-start | bytes 655360 | tf_op jit(solution)/shard_map/psum | solution.py:166
  276.1 189.1 %copy-start.36 = (pred[2,12]{0,1:T(8,128)(4,1)S(1)}, pred[2,12]{0,1:T(8,128)(4,1)}, u32[]{:S(2)}) copy-start(pred[2,12]{0,1:T(8,128)(4,1)} %broadcast_compare_fusion) | copy-start | bytes 76
  398.6 67.3 %copy-start.5 = (f32[2,27,512]{2,0,1:T(2,128)S(1)}, f32[2,27,512]{2,0,1:T(2,128)}, u32[]{:S(2)}) copy-start(f32[2,27,512]{2,0,1:T(2,128)} %param.19) | copy-start | bytes 331780
  398.6 67.3 %copy-start.7 = (f32[2,27,512]{2,0,1:T(2,128)S(1)}, f32[2,27,512]{2,0,1:T(2,128)}, u32[]{:S(2)}) copy-start(f32[2,27,512]{2,0,1:T(2,128)} %param.18) | copy-start | bytes 331780
  398.6 67.3 %copy-start.9 = (f32[2,27,512]{2,0,1:T(2,128)S(1)}, f32[2,27,512]{2,0,1:T(2,128)}, u32[]{:S(2)}) copy-start(f32[2,27,512]{2,0,1:T(2,128)} %param.20) | copy-start | bytes 331780
  467.6 184.5 %all-gather.4.cloned.1.call-start = ((), (), s32[]{:S(2)}) async-start(), calls=%async_computation.4 | async-start | bytes 2949120 | tf_op jit(solution)/shard_map/all_gather | solution.py:87
  489.0 94.9 %copy-start.35 = (bf16[64,4,18,1,7,2]{0,4,5,2,1,3:T(8,128)(2,1)S(1)}, bf16[64,4,18,1,7,2]{0,4,5,2,1,3:T(8,128)(2,1)}, u32[]{:S(2)}) copy-start(bf16[64,4,18,1,7,2]{0,4,5,2,1,3:T(8,128)(2,1)} %slice.242) | copy-start | bytes 387076
  598.8 14.8 %collective-permute-start.8 = (bf16[64,1,16,128]{3,2,1,0:T(8,128)(2,1)S(1)}, bf16[64,1,16,128]{3,2,1,0:T(8,128)(2,1)}, u32[]{:S(2)}, u32[]{:S(2)}) collective-permute-start(bf16[64,1,16,128]{3,2,1,0:T(8,128)(2,1)S(1)} %get-tuple-element.76), channel_id=1, source_target_pairs={{0,1},{1,2},{2,3},{3,4},{4,5},{5,6},{6,7},{7,0},{8,9},{9,10},{10,1... | collective-permute-start | bytes 786440 | tf_op jit(solution)/shard_map/ppermute | solution.py:22
  601.7 14.7 %collective-permute-start.9 = (bf16[64,1,16,128]{3,2,1,0:T(8,128)(2,1)S(1)}, bf16[64,1,16,128]{3,2,1,0:T(8,128)(2,1)}, u32[]{:S(2)}, u32[]{:S(2)}) collective-permute-start(bf16[64,1,16,128]{3,2,1,0:T(8,128)(2,1)S(1)} %get-tuple-element.77), channel_id=1, source_target_pairs={{1,0},{2,1},{3,2},{4,3},{5,4},{6,5},{7,6},{0,7},{9,8},{10,9},{11,1... | collective-permute-start | bytes 786440 | tf_op jit(solution)/shard_map/ppermute | solution.py:25
  (30 other events, 82.7 us)
Sparse Core Ops, SparseCore 0:
  28.8 86.7 reduce-scatter.1
  260.2 83.8 all-reduce.8
  346.5 116.2 all-reduce.4
  467.7 116.0 all-reduce.6
  586.0 66.0 all-gather.3
